TPU v7x, 128 devices: a whole 4x4x4 slice. The times are simulated.
128 devices in a mesh: row: 8 (over z, core), col: 8 (over y_hi, x), dp: 2 (over y_lo).
Axes of the slice: x: 4, y: 4 (y_hi: 2, y_lo: 2; y = y_hi * 2 + y_lo), z: 4, core: 2. Of those that a mesh axis runs over, the one named last changes fastest.
Arguments:
- tokens: bfloat16 [2048, 4096], P(('col', 'dp'), 'row'), may hold values from -6 to 6
- timesteps: int32 [8], replicated, may hold values from 0 to 999
- ada_weight: bfloat16 [3, 4096, 4096], P(None, 'col', 'row'), may hold values from -0.09375 to 0.09375
- up_weight: bfloat16 [4096, 16384], P('row', 'col'), may hold values from -0.90625 to 0.90625
- down_weight: bfloat16 [16384, 4096], P('col', 'row'), may hold values from -0.046875 to 0.046875
- cotangent: bfloat16 [2048, 4096], P(('col', 'dp'), 'row'), may hold values from -6 to 6
Outputs:
- grad_tokens: bfloat16 [2048, 4096], P(('col', 'dp'), 'row')
- grad_ada: float32 [3, 4096, 4096], P(None, 'col', 'row')
- grad_up: float32 [4096, 16384], P('row', ('col', 'dp'))
- grad_down: float32 [16384, 4096], P(('col', 'dp'), 'row')
All inputs are finite; a program needn't handle non-finite values.
Results may differ from a plain program's by a relative error of at most 0.04.
Values may be sent and summed in bfloat16 or wider, within the bound.
No kernel may reach another device: no remote copies, remote signals or barrier semaphores. Data moves between devices by JAX's collectives and lax.ppermute only.
A program may use at most 128 MiB of HBM per device.

v0:
```python
import math
import jax
import jax.numpy as jnp
from jax import lax
from jax.sharding import PartitionSpec as P

tanh_scale = math.sqrt(2.0 / math.pi)


def gelu_tanh(h):
    return 0.5 * h * (1.0 + jnp.tanh(tanh_scale * (h + 0.044715 * h * h * h)))


def gelu_slope(h):
    inner = jnp.tanh(tanh_scale * (h + 0.044715 * h * h * h))
    return 0.5 * (1.0 + inner) + 0.5 * h * (1.0 - inner * inner) * tanh_scale * (
        1.0 + 3.0 * 0.044715 * h * h
    )


def time_features(timesteps, width):
    half = width // 2
    freqs = jnp.exp(-math.log(10000.0) * jnp.arange(half, dtype=jnp.float32) / half)
    angles = timesteps.astype(jnp.float32)[:, None] * freqs[None, :]
    embed = jnp.concatenate([jnp.cos(angles), jnp.sin(angles)], axis=1)
    return jax.nn.silu(embed).astype(jnp.bfloat16)


def body(tokens, timesteps, ada_weight, up_weight, down_weight, cotangent):
    rows_count = lax.axis_size("row")
    cols_count = lax.axis_size("col")
    col_index = lax.axis_index("col")
    tok_rows, width = tokens.shape
    full_width = width * rows_count
    in_width = ada_weight.shape[1]
    cond = time_features(timesteps, full_width)
    cond_part = lax.dynamic_slice_in_dim(cond, col_index * in_width, in_width, 1)
    mod_terms = jnp.einsum("vi,kio->vko", cond_part, ada_weight, preferred_element_type=jnp.float32)
    mod = lax.psum(mod_terms.astype(jnp.bfloat16), "col").astype(jnp.float32)
    own_mod = lax.dynamic_index_in_dim(mod, col_index, 0, keepdims=False)
    shift = own_mod[0]
    scale = own_mod[1]
    gate = own_mod[2]
    x = tokens.astype(jnp.float32)
    total, squares = lax.psum((jnp.sum(x, axis=1), jnp.sum(x * x, axis=1)), "row")
    mean = total / full_width
    var = squares / full_width - mean * mean
    rstd = lax.rsqrt(var + 1e-06)
    normed = (x - mean[:, None]) * rstd[:, None]
    modulated = (normed * (1.0 + scale) + shift).astype(jnp.bfloat16)
    mod_full = lax.all_gather(modulated, "col", axis=0, tiled=True)
    picked = mod_full
    hidden_own = lax.psum_scatter(
        jnp.dot(picked, up_weight, preferred_element_type=jnp.float32).astype(jnp.bfloat16),
        "row",
        scatter_dimension=0,
        tiled=True,
    ).astype(jnp.float32)
    act_own = gelu_tanh(hidden_own).astype(jnp.bfloat16)
    act_full = lax.all_gather(act_own, "row", axis=0, tiled=True)
    picked = act_full
    branch = lax.psum_scatter(
        jnp.dot(picked, down_weight, preferred_element_type=jnp.float32).astype(jnp.bfloat16),
        "col",
        scatter_dimension=0,
        tiled=True,
    ).astype(jnp.float32)
    cot = cotangent.astype(jnp.float32)
    grad_branch = (cot * gate).astype(jnp.bfloat16)
    grad_gate = jnp.sum(cot * branch, axis=0)
    branch_full = lax.all_gather(grad_branch, "col", axis=0, tiled=True)
    mod_full = lax.all_gather(modulated, "col", axis=0, tiled=True)
    act_full = lax.all_gather(act_own, "row", axis=0, tiled=True)
    down_part = lax.dot_general(
        act_full, branch_full, (((0,), (0,)), ((), ())), preferred_element_type=jnp.float32
    )
    picked = branch_full
    grad_act = lax.psum_scatter(
        lax.dot_general(
            picked, down_weight, (((1,), (1,)), ((), ())), preferred_element_type=jnp.float32
        ).astype(jnp.bfloat16),
        "row",
        scatter_dimension=0,
        tiled=True,
    ).astype(jnp.float32)
    grad_hidden = (grad_act * gelu_slope(hidden_own)).astype(jnp.bfloat16)
    grad_full = lax.all_gather(grad_hidden, "row", axis=0, tiled=True)
    up_part = lax.dot_general(
        mod_full, grad_full, (((0,), (0,)), ((), ())), preferred_element_type=jnp.float32
    )
    picked = grad_full
    grad_mod_in = lax.psum_scatter(
        lax.dot_general(
            picked, up_weight, (((1,), (1,)), ((), ())), preferred_element_type=jnp.float32
        ).astype(jnp.bfloat16),
        "col",
        scatter_dimension=0,
        tiled=True,
    ).astype(jnp.float32)
    grad_up, grad_down = (
        lax.psum_scatter(
            up_part.astype(jnp.bfloat16), "dp", scatter_dimension=1, tiled=True
        ).astype(jnp.float32),
        lax.psum_scatter(
            down_part.astype(jnp.bfloat16), "dp", scatter_dimension=0, tiled=True
        ).astype(jnp.float32),
    )
    grad_norm = grad_mod_in * (1.0 + scale)
    first, second = lax.psum(
        (jnp.sum(grad_norm, axis=1), jnp.sum(grad_norm * normed, axis=1)), "row"
    )
    first = first / full_width
    second = second / full_width
    grad_tokens = cot + rstd[:, None] * (grad_norm - first[:, None] - normed * second[:, None])
    own_grad = jnp.stack(
        [jnp.sum(grad_mod_in, axis=0), jnp.sum(grad_mod_in * normed, axis=0), grad_gate], axis=0
    )
    selector = (jnp.arange(cols_count, dtype=jnp.int32) == col_index).astype(jnp.float32)
    placed = selector[:, None, None] * own_grad[None, :, :]
    grad_mod = lax.psum(placed.astype(jnp.bfloat16), ("col", "dp")).astype(jnp.float32)
    grad_ada = jnp.einsum(
        "vi,vko->kio", cond_part.astype(jnp.float32), grad_mod, precision=lax.Precision.HIGHEST
    )
    return (grad_tokens.astype(jnp.bfloat16), grad_ada, grad_up, grad_down)


def solution(mesh):
    return jax.shard_map(
        body,
        mesh=mesh,
        in_specs=(
            P(("col", "dp"), "row"),
            P(),
            P(None, "col", "row"),
            P("row", "col"),
            P("col", "row"),
            P(("col", "dp"), "row"),
        ),
        out_specs=(
            P(("col", "dp"), "row"),
            P(None, "col", "row"),
            P("row", ("col", "dp")),
            P(("col", "dp"), "row"),
        ),
        check_vma=False,
    )
```

profile of v0, /device:TPU:0, one launch (start us, length us, event | category | flops | bytes accessed | tf_op | source)
XLA Modules:
  0.0 550.7 jit_solution(17362788977848606605)
XLA Ops:
  7.2 0.0 all-gather.7.cloned.1.call-start
  7.3 0.8 convert_element_type.83
  8.1 1.0 fusion.20
  9.1 0.3 multiply_cosine_fusion
  9.4 1.7 convolution_convert_fusion.6
  11.1 42.0 %psum.44 = bf16[8,3,512]{2,0,1:T(8,128)(2,1)S(1)} all-reduce(bf16[8,3,512]{2,0,1:T(8,128)(2,1)S(1)} %convolution_convert_fusion.6), channel_id=1, replica_groups=mesh['row'=8,'col'=8,'dp'=2] {'col'}, use_global_device_ids=true, to_apply=%region_4.5 | all-reduce | flops 12288 | bytes 49152 | tf_op jit(solution)/shard_map/psum | solution.py:39
  53.2 13.1 %all-reduce.1 = (f32[128]{0:T(128)S(1)}, f32[128]{0:T(128)S(1)}) all-reduce(f32[128]{0:T(128)S(1)} %get-tuple-element.13, f32[128]{0:T(128)S(1)} %get-tuple-element.12), channel_id=1, replica_groups=mesh['row'=8,'col'=8,'dp'=2] {'row'}, use_global_device_ids=true, to_apply=%region_3.4 | all-reduce | flops 256 | bytes 2048 | tf_op jit(solution)/shard_map/psum | solution.py:45
  66.3 0.8 fusion.25
  67.1 0.0 all-gather.7.cloned.1.call-update
  67.1 0.0 all-gather.5.cloned.1.call-start
  67.2 0.7 fusion.17
  67.9 0.0 all-gather.5.cloned.1.call-update
  67.9 0.0 reduce-scatter.9.cloned.1.call-start
  68.0 41.2 %all-gather.7.cloned.1.call-done = bf16[1024,512]{1,0:T(8,128)(2,1)} async-done(((bf16[128,512]{1,0:T(8,128)(2,1)}), bf16[1024,512]{1,0:T(8,128)(2,1)}) %all-gather.7.cloned.1.call-update) | async-done | bytes 1048592 | tf_op jit(solution)/shard_map/all_gather | solution.py:51
  109.1 5.5 convolution_convert_fusion
  114.7 0.0 reduce-scatter.7.cloned.1.call-start
  114.7 43.4 %all-gather.5.cloned.1.call-done = bf16[1024,512]{1,0:T(8,128)(2,1)} async-done(((bf16[128,512]{1,0:T(8,128)(2,1)}), bf16[1024,512]{1,0:T(8,128)(2,1)}) %all-gather.5.cloned.1.call-update) | async-done | bytes 1048592 | tf_op jit(solution)/shard_map/all_gather | solution.py:71
  158.1 6.3 %convolution_convert_fusion.1 = bf16[1024,2048]{1,0:T(8,128)(2,1)} fusion(bf16[1024,512]{1,0:T(8,128)(2,1)} %all-gather.5.cloned.1.call-done, bf16[2048,512]{1,0:T(8,128)(2,1)} %param.10), kind=kOutput, calls=%fused_computation.1 | convolution fusion | flops 2149580800 | bytes 7340032 | tf_op jit(solution)/shard_map/dot_general | solution.py:79
  164.4 0.0 reduce-scatter.7.cloned.1.call-update
  164.4 0.0 all-gather.9.cloned.1.call-start
  164.5 33.3 %reduce-scatter.9.cloned.1.call-done = bf16[128,2048]{1,0:T(8,128)(2,1)} async-done(((bf16[1024,2048]{1,0:T(8,128)(2,1)}), bf16[128,2048]{1,0:T(8,128)(2,1)}) %reduce-scatter.9.cloned.1.call-update) | async-done | bytes 524304 | tf_op jit(solution)/shard_map/reduce_scatter | solution.py:53
  197.7 39.2 %reduce-scatter.7.cloned.1.call-done = bf16[128,2048]{1,0:T(8,128)(2,1)} async-done(((bf16[1024,2048]{1,0:T(8,128)(2,1)}), bf16[128,2048]{1,0:T(8,128)(2,1)}) %reduce-scatter.7.cloned.1.call-update) | async-done | bytes 524304 | tf_op jit(solution)/shard_map/reduce_scatter | solution.py:78
  237.0 2.9 fusion.7
  239.9 0.0 all-gather.9.cloned.1.call-update
  240.0 0.0 all-gather.11.cloned.1.call-start
  240.0 0.5 all-gather.11.cloned.1.call-update
  240.5 0.0 reduce-scatter.11.cloned.1.call-start
  240.6 30.5 %all-gather.9.cloned.1.call-done = bf16[1024,2048]{1,0:T(8,128)(2,1)} async-done(((bf16[128,2048]{1,0:T(8,128)(2,1)}), bf16[1024,2048]{1,0:T(8,128)(2,1)}) %all-gather.9.cloned.1.call-update) | async-done | bytes 4194320 | tf_op jit(solution)/shard_map/all_gather | solution.py:87
  271.1 5.5 %convolution_convert_fusion.5 = bf16[1024,512]{1,0:T(8,128)(2,1)} fusion(bf16[1024,2048]{1,0:T(8,128)(2,1)} %all-gather.9.cloned.1.call-done, bf16[512,2048]{1,0:T(8,128)(2,1)S(1)} %copy-done), kind=kOutput, calls=%fused_computation.13 | convolution fusion | flops 2148007936 | bytes 7340032 | tf_op jit(solution)/shard_map/dot_general | solution.py:93
  276.7 0.0 reduce-scatter.13.cloned.1.call-start
  276.7 28.6 %all-gather.11.cloned.1.call-done = bf16[1024,2048]{1,0:T(8,128)(2,1)} async-done(((bf16[128,2048]{1,0:T(8,128)(2,1)}), bf16[1024,2048]{1,0:T(8,128)(2,1)}) %all-gather.11.cloned.1.call-update) | async-done | bytes 4194320 | tf_op jit(solution)/shard_map/all_gather | solution.py:60
  305.4 6.2 %convolution_convert_fusion.4 = bf16[1024,512]{1,0:T(8,128)(2,1)} fusion(bf16[1024,2048]{1,0:T(8,128)(2,1)} %all-gather.11.cloned.1.call-done, bf16[2048,512]{1,0:T(8,128)(2,1)} %param.10), kind=kOutput, calls=%fused_computation.12 | convolution fusion | flops 2148007936 | bytes 7340032 | tf_op jit(solution)/shard_map/dot_general | solution.py:63
  311.6 0.0 reduce-scatter.15.cloned.1.call-start
  311.6 5.9 %convolution_convert_fusion.3 = bf16[512,2048]{1,0:T(8,128)(2,1)} fusion(bf16[1024,512]{1,0:T(8,128)(2,1)S(1)} %copy-done.3, bf16[1024,2048]{1,0:T(8,128)(2,1)} %all-gather.9.cloned.1.call-done), kind=kOutput, calls=%fused_computation.3 | convolution fusion | flops 2148532224 | bytes 7340032 | tf_op jit(solution)/shard_map/dot_general | solution.py:88
  317.6 0.2 reduce-scatter.17.cloned.1.call-start
  317.8 1.0 copy-done.4
  318.8 5.9 %convolution_convert_fusion.2 = bf16[2048,512]{1,0:T(8,128)(2,1)} fusion(bf16[1024,2048]{1,0:T(8,128)(2,1)} %all-gather.11.cloned.1.call-done, bf16[1024,512]{1,0:T(8,128)(2,1)S(1)} %copy-done.4), kind=kOutput, calls=%fused_computation.2 | convolution fusion | flops 2148532224 | bytes 7340032 | tf_op jit(solution)/shard_map/dot_general | solution.py:74
  324.7 57.5 %reduce-scatter.11.cloned.1.call-done = bf16[128,512]{1,0:T(8,128)(2,1)} async-done(((bf16[1024,512]{1,0:T(8,128)(2,1)}), bf16[128,512]{1,0:T(8,128)(2,1)}) %reduce-scatter.11.cloned.1.call-update) | async-done | bytes 131088 | tf_op jit(solution)/shard_map/reduce_scatter | solution.py:92
  382.2 1.1 fusion.26
  383.3 12.8 %all-reduce = (f32[128]{0:T(128)S(1)}, f32[128]{0:T(128)S(1)}) all-reduce(f32[128]{0:T(128)S(1)} %get-tuple-element.9, f32[128]{0:T(128)S(1)} %get-tuple-element.10), channel_id=1, replica_groups=mesh['row'=8,'col'=8,'dp'=2] {'row'}, use_global_device_ids=true, to_apply=%region_11.12 | all-reduce | flops 256 | bytes 2048 | tf_op jit(solution)/shard_map/psum | solution.py:109
  396.1 62.1 %reduce-scatter.13.cloned.1.call-done = bf16[128,512]{1,0:T(8,128)(2,1)} async-done(((bf16[1024,512]{1,0:T(8,128)(2,1)}), bf16[128,512]{1,0:T(8,128)(2,1)}) %reduce-scatter.13.cloned.1.call-update) | async-done | bytes 131088 | tf_op jit(solution)/shard_map/reduce_scatter | solution.py:62
  458.1 1.8 fusion.19
  459.9 0.1 multiply_convert_fusion
  460.0 72.4 %psum.47 = bf16[8,3,512]{2,0,1:T(8,128)(2,1)S(1)} all-reduce(bf16[8,3,512]{2,0,1:T(8,128)(2,1)S(1)} %multiply_convert_fusion), channel_id=1, replica_groups=mesh['row'=8,'col'=8,'dp'=2] {'col','dp'}, use_global_device_ids=true, to_apply=%region_16.17 | all-reduce | flops 12288 | bytes 49152 | tf_op jit(solution)/shard_map/psum | solution.py:120
  532.4 2.3 convolution_bitcast_fusion
  534.7 3.5 copy.10
  538.2 2.8 convert_element_type.103
  541.0 2.8 convert_element_type.105
  (23 shorter events, 0.2 us)
Async XLA Ops:
  7.2 102.0 %copy-start = (bf16[512,2048]{1,0:T(8,128)(2,1)S(1)}, bf16[512,2048]{1,0:T(8,128)(2,1)}, u32[]{:S(2)}) copy-start(bf16[512,2048]{1,0:T(8,128)(2,1)} %param.9) | copy-start | bytes 6291460
  7.2 59.2 %copy-start.1 = (bf16[128,512]{1,0:T(8,128)(2,1)S(1)}, bf16[128,512]{1,0:T(8,128)(2,1)}, u32[]{:S(2)}) copy-start(bf16[128,512]{1,0:T(8,128)(2,1)} %param.6) | copy-start | bytes 393220
  7.2 60.0 %copy-start.2 = (bf16[128,512]{1,0:T(8,128)(2,1)S(1)}, bf16[128,512]{1,0:T(8,128)(2,1)}, u32[]{:S(2)}) copy-start(bf16[128,512]{1,0:T(8,128)(2,1)} %param.11) | copy-start | bytes 393220
  7.2 101.9 %all-gather.7.cloned.1.call-start = ((), (), s32[]{:S(2)}) async-start(), calls=%async_computation.8 | async-start | bytes 1179648 | tf_op jit(solution)/shard_map/all_gather | solution.py:51
  67.1 91.0 %all-gather.5.cloned.1.call-start = ((), (), s32[]{:S(2)}) async-start(), calls=%async_computation.6 | async-start | bytes 1179648 | tf_op jit(solution)/shard_map/all_gather | solution.py:71
  67.9 129.8 %reduce-scatter.9.cloned.1.call-start = ((), (), s32[]{:S(2)}) async-start(), calls=%async_computation.9 | async-start | bytes 4718592 | tf_op jit(solution)/shard_map/reduce_scatter | solution.py:53
  114.7 122.3 %reduce-scatter.7.cloned.1.call-start = ((), (), s32[]{:S(2)}) async-start(), calls=%async_computation.7 | async-start | bytes 4718592 | tf_op jit(solution)/shard_map/reduce_scatter | solution.py:78
  164.4 106.7 %all-gather.9.cloned.1.call-start = ((), (), s32[]{:S(2)}) async-start(), calls=%async_computation.10 | async-start | bytes 4718592 | tf_op jit(solution)/shard_map/all_gather | solution.py:87
  240.0 65.4 %all-gather.11.cloned.1.call-start = ((), (), s32[]{:S(2)}) async-start(), calls=%async_computation.12 | async-start | bytes 4718592 | tf_op jit(solution)/shard_map/all_gather | solution.py:60
  240.5 141.7 %reduce-scatter.11.cloned.1.call-start = ((), (), s32[]{:S(2)}) async-start(), calls=%async_computation.11 | async-start | bytes 1179648 | tf_op jit(solution)/shard_map/reduce_scatter | solution.py:92
  276.7 34.9 %copy-start.3 = (bf16[1024,512]{1,0:T(8,128)(2,1)S(1)}, bf16[1024,512]{1,0:T(8,128)(2,1)}, u32[]{:S(2)}) copy-start(bf16[1024,512]{1,0:T(8,128)(2,1)} %all-gather.7.cloned.1.call-done) | copy-start | bytes 3145732
  276.7 181.5 %reduce-scatter.13.cloned.1.call-start = ((), (), s32[]{:S(2)}) async-start(), calls=%async_computation.13 | async-start | bytes 1179648 | tf_op jit(solution)/shard_map/reduce_scatter | solution.py:62
  311.6 226.6 %reduce-scatter.15.cloned.1.call-start = ((), (), s32[]{:S(2)}) async-start(), calls=%async_computation.14 | async-start | bytes 3145728 | tf_op jit(solution)/shard_map/reduce_scatter | solution.py:101
  317.5 1.2 copy-start.4
  317.6 223.4 %reduce-scatter.17.cloned.1.call-start = ((), (), s32[]{:S(2)}) async-start(), calls=%async_computation.15 | async-start | bytes 3145728 | tf_op jit(solution)/shard_map/reduce_scatter | solution.py:104
Sparse Core Ops, SparseCore 0:
  67.3 41.8 all-gather.6
  112.0 46.0 all-gather.4
  160.5 37.1 reduce-scatter.8
  200.0 36.9 reduce-scatter.6
  240.1 31.0 all-gather.8
  273.3 32.0 all-gather.10
  309.6 72.5 reduce-scatter.10
  386.4 71.6 reduce-scatter.12
  461.1 33.8 reduce-scatter.14
  497.1 36.2 reduce-scatter.16
where the time goes:
time: 551 us
  waiting for transfers between devices  336 us (61%)
  blocking collectives  140 us (25%)
  matrix products  39.3 us (7%)
  other arithmetic  15.2 us (3%)
  between operations  14.3 us (3%)
    psum x1, blocking collectives, body(): lax.psum(placed.astype(jnp.bfloat16), ('col', 'dp')).astype(jnp.float32)  72.4 us
    reduce_scatter x1, waiting for transfers between devices, body(): lax.psum_scatter(jnp.dot(picked, down_weight, preferred_element_type=jnp....  62.1 us
    reduce_scatter x1, waiting for transfers between devices, body(): lax.psum_scatter(lax.dot_general(picked, up_weight, (((1,), (1,)), ((), (...  57.5 us
    all_gather x1, waiting for transfers between devices, body(): branch_full = lax.all_gather(grad_branch, 'col', axis=0, tiled=True)  43.4 us
    psum x1, blocking collectives, body(): mod = lax.psum(mod_terms.astype(jnp.bfloat16), 'col').astype(jnp.float32)  42 us
    all_gather x1, waiting for transfers between devices, body(): mod_full = lax.all_gather(modulated, 'col', axis=0, tiled=True)  41.2 us
    reduce_scatter x1, waiting for transfers between devices, body(): lax.psum_scatter(lax.dot_general(picked, down_weight, (((1,), (1,)), ((),...  39.2 us
    reduce_scatter x1, waiting for transfers between devices, body(): lax.psum_scatter(jnp.dot(picked, up_weight, preferred_element_type=jnp.fl...  33.3 us
  transfers between devices with their start and end apart: 10, of which 8 were waited for; matrix products, arithmetic and copies ran while one was open for 9% of the time, Pallas kernels for 0%

commit v1 on v0

--- a/solution.py
+++ b/solution.py
@@ -84,7 +84,9 @@
         tiled=True,
     ).astype(jnp.float32)
     grad_hidden = (grad_act * gelu_slope(hidden_own)).astype(jnp.bfloat16)
-    grad_full = lax.all_gather(grad_hidden, "row", axis=0, tiled=True)
+    grad_full = jnp.concatenate(
+        lax.all_to_all(jnp.stack([grad_hidden] * lax.axis_size("row")), "row", 0, 0), axis=0
+    )
     up_part = lax.dot_general(
         mod_full, grad_full, (((0,), (0,)), ((), ())), preferred_element_type=jnp.float32
     )

time: 551 us -> 592 us (1.074)
  blocking collectives: 140 us -> 209 us
  waiting for transfers between devices: 336 us -> 307 us
    all_to_all x0 -> x1, blocking collectives: none -> 69.1 us  [body(): lax.all_to_all(jnp.stack([grad_hidden] * lax.axis_size('row')), 'row', 0, 0)]
    all_gather x1 -> x0, waiting for transfers between devices: 30.5 us -> none  [body(): grad_full = lax.all_gather(grad_hidden, 'row', axis=0, tiled=True)]
    all_gather x1, waiting for transfers between devices: 28.6 us -> 0.02 us  [body(): act_full = lax.all_gather(act_own, 'row', axis=0, tiled=True)]
    reduce_scatter x1, waiting for transfers between devices: 0.01 us -> 22.4 us  [body(): lax.psum_scatter(up_part.astype(jnp.bfloat16), 'dp', scatter_dimension=1,...]
    reduce_scatter x1, waiting for transfers between devices: 62.1 us -> 75.2 us  [body(): lax.psum_scatter(jnp.dot(picked, down_weight, preferred_element_type=jnp....]
  transfers between devices with their start and end apart: 10 -> 9, of which waited for: 8 -> 7; matrix products, arithmetic and copies ran while one was open for 9% -> 8% of each run, Pallas kernels for 0% -> 0%
where the time goes in v1:
time: 592 us; the launch traced here: 591 us
  waiting for transfers between devices  307 us (52%)
  blocking collectives  209 us (35%)
  matrix products  37.8 us (6%)
  other arithmetic  16.8 us (3%)
  between operations  13.9 us (2%)
  local copies, waits for them, and re-layouts  6.04 us (1%)
    reduce_scatter x1, waiting for transfers between devices, body(): lax.psum_scatter(jnp.dot(picked, down_weight, preferred_element_type=jnp....  75.2 us
    psum x1, blocking collectives, body(): lax.psum(placed.astype(jnp.bfloat16), ('col', 'dp')).astype(jnp.float32)  72.4 us
    all_to_all x1, blocking collectives, body(): lax.all_to_all(jnp.stack([grad_hidden] * lax.axis_size('row')), 'row', 0, 0)  69.1 us
    reduce_scatter x1, waiting for transfers between devices, body(): lax.psum_scatter(lax.dot_general(picked, up_weight, (((1,), (1,)), ((), (...  53 us
    all_gather x1, waiting for transfers between devices, body(): branch_full = lax.all_gather(grad_branch, 'col', axis=0, tiled=True)  43.4 us
    psum x1, blocking collectives, body(): mod = lax.psum(mod_terms.astype(jnp.bfloat16), 'col').astype(jnp.float32)  42 us
    all_gather x1, waiting for transfers between devices, body(): mod_full = lax.all_gather(modulated, 'col', axis=0, tiled=True)  40.3 us
    reduce_scatter x1, waiting for transfers between devices, body(): lax.psum_scatter(lax.dot_general(picked, down_weight, (((1,), (1,)), ((),...  39.2 us
  transfers between devices with their start and end apart: 9, of which 7 were waited for; matrix products, arithmetic and copies ran while one was open for 8% of the time, Pallas kernels for 0%

profile of v1, /device:TPU:0, one launch (start us, length us, event | category | flops | bytes accessed | tf_op | source)
XLA Modules:
  0.0 591.5 jit_solution(8614548376918555776)
XLA Ops:
  7.2 0.0 all-gather.6.cloned.1.call-start
  7.2 0.8 convert_element_type.83
  8.0 1.0 fusion.20
  9.1 0.3 multiply_cosine_fusion
  9.4 1.7 convolution_convert_fusion.6
  11.1 42.0 %psum.44 = bf16[8,3,512]{2,0,1:T(8,128)(2,1)S(1)} all-reduce(bf16[8,3,512]{2,0,1:T(8,128)(2,1)S(1)} %convolution_convert_fusion.6), channel_id=1, replica_groups=mesh['row'=8,'col'=8,'dp'=2] {'col'}, use_global_device_ids=true, to_apply=%region_4.5 | all-reduce | flops 12288 | bytes 49152 | tf_op jit(solution)/shard_map/psum | solution.py:39
  53.2 13.1 %all-reduce.1 = (f32[128]{0:T(128)S(1)}, f32[128]{0:T(128)S(1)}) all-reduce(f32[128]{0:T(128)S(1)} %get-tuple-element.13, f32[128]{0:T(128)S(1)} %get-tuple-element.12), channel_id=1, replica_groups=mesh['row'=8,'col'=8,'dp'=2] {'row'}, use_global_device_ids=true, to_apply=%region_3.4 | all-reduce | flops 256 | bytes 2048 | tf_op jit(solution)/shard_map/psum | solution.py:45
  66.3 1.7 fusion.25
  68.0 0.0 all-gather.6.cloned.1.call-update
  68.0 0.0 all-gather.4.cloned.1.call-start
  68.1 1.6 fusion.17
  69.7 0.0 all-gather.4.cloned.1.call-update
  69.7 0.0 reduce-scatter.9.cloned.1.call-start
  69.7 40.3 %all-gather.6.cloned.1.call-done = bf16[1024,512]{1,0:T(8,128)(2,1)} async-done(((bf16[128,512]{1,0:T(8,128)(2,1)}), bf16[1024,512]{1,0:T(8,128)(2,1)}) %all-gather.6.cloned.1.call-update) | async-done | bytes 1048592 | tf_op jit(solution)/shard_map/all_gather | solution.py:51
  110.0 5.5 convolution_convert_fusion
  115.5 0.0 reduce-scatter.9.cloned.1.call-update
  115.5 0.0 reduce-scatter.7.cloned.1.call-start
  115.6 43.4 %all-gather.4.cloned.1.call-done = bf16[1024,512]{1,0:T(8,128)(2,1)} async-done(((bf16[128,512]{1,0:T(8,128)(2,1)}), bf16[1024,512]{1,0:T(8,128)(2,1)}) %all-gather.4.cloned.1.call-update) | async-done | bytes 1048592 | tf_op jit(solution)/shard_map/all_gather | solution.py:71
  159.0 6.3 %convolution_convert_fusion.1 = bf16[1024,2048]{1,0:T(8,128)(2,1)} fusion(bf16[1024,512]{1,0:T(8,128)(2,1)} %all-gather.4.cloned.1.call-done, bf16[2048,512]{1,0:T(8,128)(2,1)} %param.10), kind=kOutput, calls=%fused_computation.1 | convolution fusion | flops 2149580800 | bytes 7340032 | tf_op jit(solution)/shard_map/dot_general | solution.py:79
  165.3 0.0 all-gather.8.cloned.1.call-start
  165.3 33.3 %reduce-scatter.9.cloned.1.call-done = bf16[128,2048]{1,0:T(8,128)(2,1)} async-done(((bf16[1024,2048]{1,0:T(8,128)(2,1)}), bf16[128,2048]{1,0:T(8,128)(2,1)}) %reduce-scatter.9.cloned.1.call-update) | async-done | bytes 524304 | tf_op jit(solution)/shard_map/reduce_scatter | solution.py:53
  198.6 39.2 %reduce-scatter.7.cloned.1.call-done = bf16[128,2048]{1,0:T(8,128)(2,1)} async-done(((bf16[1024,2048]{1,0:T(8,128)(2,1)}), bf16[128,2048]{1,0:T(8,128)(2,1)}) %reduce-scatter.7.cloned.1.call-update) | async-done | bytes 524304 | tf_op jit(solution)/shard_map/reduce_scatter | solution.py:78
  237.8 2.8 fusion.7
  240.6 0.0 reduce-scatter.11.cloned.1.call-start
  240.7 0.5 stack.10
  241.2 69.1 %all_to_all.5 = bf16[8,128,2048]{2,1,0:T(8,128)(2,1)S(1)} all-to-all(bf16[8,128,2048]{2,1,0:T(8,128)(2,1)S(1)} %stack.10), channel_id=1, replica_groups=mesh['row'=8,'col'=8,'dp'=2] {'row'}, dimensions={0} | all-to-all | bytes 8388608 | tf_op jit(solution)/shard_map/all_to_all | solution.py:88
  310.3 2.0 copy-done.1
  312.2 3.4 convolution_convert_fusion.5
  315.6 0.0 reduce-scatter.11.cloned.1.call-update
  315.6 0.0 reduce-scatter.15.cloned.1.call-start
  315.7 6.2 %convolution_convert_fusion.3 = bf16[512,2048]{1,0:T(8,128)(2,1)} fusion(bf16[1024,512]{1,0:T(8,128)(2,1)} %all-gather.6.cloned.1.call-done, bf16[1024,2048]{1,0:T(8,128)(2,1)} %bitcast.29), kind=kOutput, calls=%fused_computation.3 | convolution fusion | flops 2148532224 | bytes 7340032 | tf_op jit(solution)/shard_map/dot_general | solution.py:90
  321.9 0.2 reduce-scatter.13.cloned.1.call-start
  322.1 0.0 all-gather.8.cloned.1.call-done
  322.2 6.3 %convolution_convert_fusion.4 = bf16[1024,512]{1,0:T(8,128)(2,1)} fusion(bf16[1024,2048]{1,0:T(8,128)(2,1)} %all-gather.8.cloned.1.call-done, bf16[2048,512]{1,0:T(8,128)(2,1)} %param.10), kind=kOutput, calls=%fused_computation.12 | convolution fusion | flops 2148007936 | bytes 7340032 | tf_op jit(solution)/shard_map/dot_general | solution.py:63
  328.5 0.0 reduce-scatter.17.cloned.1.call-start
  328.5 6.2 %convolution_convert_fusion.2 = bf16[2048,512]{1,0:T(8,128)(2,1)} fusion(bf16[1024,2048]{1,0:T(8,128)(2,1)} %all-gather.8.cloned.1.call-done, bf16[1024,512]{1,0:T(8,128)(2,1)} %all-gather.4.cloned.1.call-done), kind=kOutput, calls=%fused_computation.2 | convolution fusion | flops 2148532224 | bytes 7340032 | tf_op jit(solution)/shard_map/dot_general | solution.py:74
  334.8 53.0 %reduce-scatter.11.cloned.1.call-done = bf16[128,512]{1,0:T(8,128)(2,1)} async-done(((bf16[1024,512]{1,0:T(8,128)(2,1)}), bf16[128,512]{1,0:T(8,128)(2,1)}) %reduce-scatter.11.cloned.1.call-update) | async-done | bytes 131088 | tf_op jit(solution)/shard_map/reduce_scatter | solution.py:94
  387.8 1.2 fusion.26
  389.0 12.8 %all-reduce = (f32[128]{0:T(128)S(1)}, f32[128]{0:T(128)S(1)}) all-reduce(f32[128]{0:T(128)S(1)} %get-tuple-element.9, f32[128]{0:T(128)S(1)} %get-tuple-element.10), channel_id=1, replica_groups=mesh['row'=8,'col'=8,'dp'=2] {'row'}, use_global_device_ids=true, to_apply=%region_11.12 | all-reduce | flops 256 | bytes 2048 | tf_op jit(solution)/shard_map/psum | solution.py:111
  401.7 22.4 %reduce-scatter.15.cloned.1.call-done = bf16[512,1024]{1,0:T(8,128)(2,1)} async-done(((bf16[512,2048]{1,0:T(8,128)(2,1)}), bf16[512,1024]{1,0:T(8,128)(2,1)}) %reduce-scatter.15.cloned.1.call-update) | async-done | bytes 1048592 | tf_op jit(solution)/shard_map/reduce_scatter | solution.py:103
  424.1 2.8 convert_element_type.103
  426.9 75.2 %reduce-scatter.13.cloned.1.call-done = bf16[128,512]{1,0:T(8,128)(2,1)} async-done(((bf16[1024,512]{1,0:T(8,128)(2,1)}), bf16[128,512]{1,0:T(8,128)(2,1)}) %reduce-scatter.13.cloned.1.call-update) | async-done | bytes 131088 | tf_op jit(solution)/shard_map/reduce_scatter | solution.py:62
  502.1 1.7 fusion.19
  503.9 0.1 multiply_convert_fusion
  503.9 72.4 %psum.47 = bf16[8,3,512]{2,0,1:T(8,128)(2,1)S(1)} all-reduce(bf16[8,3,512]{2,0,1:T(8,128)(2,1)S(1)} %multiply_convert_fusion), channel_id=1, replica_groups=mesh['row'=8,'col'=8,'dp'=2] {'col','dp'}, use_global_device_ids=true, to_apply=%region_16.17 | all-reduce | flops 12288 | bytes 49152 | tf_op jit(solution)/shard_map/psum | solution.py:122
  576.3 2.3 convolution_bitcast_fusion
  578.6 3.5 copy.10
  582.1 2.8 convert_element_type.105
  (22 shorter events, 0.2 us)
Async XLA Ops:
  7.2 102.8 %copy-start = (bf16[512,2048]{1,0:T(8,128)(2,1)S(1)}, bf16[512,2048]{1,0:T(8,128)(2,1)}, u32[]{:S(2)}) copy-start(bf16[512,2048]{1,0:T(8,128)(2,1)} %param.9) | copy-start | bytes 6291460
  7.2 102.8 %all-gather.6.cloned.1.call-start = ((), (), s32[]{:S(2)}) async-start(), calls=%async_computation.9 | async-start | bytes 1179648 | tf_op jit(solution)/shard_map/all_gather | solution.py:51
  68.0 91.0 %all-gather.4.cloned.1.call-start = ((), (), s32[]{:S(2)}) async-start(), calls=%async_computation.7 | async-start | bytes 1179648 | tf_op jit(solution)/shard_map/all_gather | solution.py:71
  69.7 128.9 %reduce-scatter.9.cloned.1.call-start = ((), (), s32[]{:S(2)}) async-start(), calls=%async_computation.10 | async-start | bytes 4718592 | tf_op jit(solution)/shard_map/reduce_scatter | solution.py:53
  115.5 122.3 %reduce-scatter.7.cloned.1.call-start = ((), (), s32[]{:S(2)}) async-start(), calls=%async_computation.8 | async-start | bytes 4718592 | tf_op jit(solution)/shard_map/reduce_scatter | solution.py:78
  165.3 156.9 %all-gather.8.cloned.1.call-start = ((), (), s32[]{:S(2)}) async-start(), calls=%async_computation.12 | async-start | bytes 4718592 | tf_op jit(solution)/shard_map/all_gather | solution.py:60
  240.6 147.1 %reduce-scatter.11.cloned.1.call-start = ((), (), s32[]{:S(2)}) async-start(), calls=%async_computation.11 | async-start | bytes 1179648 | tf_op jit(solution)/shard_map/reduce_scatter | solution.py:94
  310.3 2.0 copy-start.1
  315.6 108.5 %reduce-scatter.15.cloned.1.call-start = ((), (), s32[]{:S(2)}) async-start(), calls=%async_computation.14 | async-start | bytes 3145728 | tf_op jit(solution)/shard_map/reduce_scatter | solution.py:103
  321.9 180.2 %reduce-scatter.13.cloned.1.call-start = ((), (), s32[]{:S(2)}) async-start(), calls=%async_computation.13 | async-start | bytes 1179648 | tf_op jit(solution)/shard_map/reduce_scatter | solution.py:62
  328.5 59.3 %copy-start.2 = (bf16[128,512]{1,0:T(8,128)(2,1)S(1)}, bf16[128,512]{1,0:T(8,128)(2,1)}, u32[]{:S(2)}) copy-start(bf16[128,512]{1,0:T(8,128)(2,1)} %param.6) | copy-start | bytes 393220
  328.5 253.7 %reduce-scatter.17.cloned.1.call-start = ((), (), s32[]{:S(2)}) async-start(), calls=%async_computation.15 | async-start | bytes 3145728 | tf_op jit(solution)/shard_map/reduce_scatter | solution.py:106
  334.8 167.3 %copy-start.3 = (bf16[128,512]{1,0:T(8,128)(2,1)S(1)}, bf16[128,512]{1,0:T(8,128)(2,1)}, u32[]{:S(2)}) copy-start(bf16[128,512]{1,0:T(8,128)(2,1)} %param.11) | copy-start | bytes 393220
  387.8 114.3 %copy-start.4 = (bf16[128,512]{1,0:T(8,128)(2,1)S(1)}, bf16[128,512]{1,0:T(8,128)(2,1)}, u32[]{:S(2)}) copy-start(bf16[128,512]{1,0:T(8,128)(2,1)} %reduce-scatter.11.cloned.1.call-done) | copy-start | bytes 393220
Sparse Core Ops, SparseCore 0:
  68.1 41.8 all-gather.5
  112.9 46.0 all-gather.3
  161.4 37.1 reduce-scatter.8
  200.9 36.9 reduce-scatter.6
  240.8 64.5 all-gather.7
  315.8 71.9 reduce-scatter.10
  390.7 33.4 reduce-scatter.14
  428.4 73.6 reduce-scatter.12
  504.5 33.8 reduce-scatter.16
